TPU v7x, 128 devices: a whole 4x4x4 slice. The times are simulated.
128 devices in a mesh: dp: 32 (over y, x, core), mp: 4 (over z).
Axes of the slice: x: 4, y: 4, z: 4, core: 2. Of those that a mesh axis runs over, the one named last changes fastest.
Arguments:
- hidden: bfloat16 [4096, 2560], P('dp', 'mp'), may hold values from -6 to 6
- norm_gain: bfloat16 [2560], replicated, may hold values from 0.5 to 1.5
- shared_gate: bfloat16 [2560, 3072], P(None, 'mp'), may hold values from -0.125 to 0.125
- shared_up: bfloat16 [2560, 3072], P(None, 'mp'), may hold values from -0.125 to 0.125
- shared_down: bfloat16 [3072, 2560], P('mp'), may hold values from -0.109375 to 0.109375
- expert_gate: bfloat16 [64, 2560, 1536], P('dp', None, 'mp'), may hold values from -0.125 to 0.125
- expert_up: bfloat16 [64, 2560, 1536], P('dp', None, 'mp'), may hold values from -0.125 to 0.125
- expert_down: bfloat16 [64, 1536, 2560], P('dp', 'mp'), may hold values from -0.15625 to 0.15625
- adapter_in: bfloat16 [64, 3072, 16], P('dp', 'mp'), may hold values from -0.109375 to 0.109375
- adapter_out: bfloat16 [64, 16, 2560], P('dp'), may hold values from -1.5 to 1.5
- active: int32 [16], replicated, may hold values from 0 to 63, as said below
- lengths: int32 [64], replicated, may hold values from 1 to 1024, 4096 in all
- request_adapter: int32 [64], replicated, may hold values from 0 to 15
- routes: int32 [4096, 6], P('dp'), may hold values from 0 to 63, all different within a row; in each aligned block of 128 rows (0 to 127, 128 to 255, ...) at most 16 rows name the same one
- route_weights: float32 [4096, 6], P('dp'), may hold values from 0.05 to 0.35
Outputs:
- layer_out: bfloat16 [4096, 2560], P('dp', 'mp')
Inputs may be any that keep to these rules, and one draw needn't show every extreme that they name: `active`: the entries are distinct. `routes`: within the 128 rows of one index of dp no expert is named more than 16 times, and that many is reached; a row names distinct experts.
All inputs are finite; a program needn't handle non-finite values.
Results may differ from a plain program's by a relative error of at most 0.015.
Values may be sent and summed in bfloat16 or wider, within the bound.
No kernel may reach another device: no remote copies, remote signals or barrier semaphores. Data moves between devices by JAX's collectives and lax.ppermute only.
A program may use at most 128 MiB of HBM per device.

v0:
```python
import jax
import jax.numpy as jnp
from jax import lax
from jax.sharding import PartitionSpec as P


def experts_apply(slots_in, expert_gate, expert_up, expert_down):
    gate_val = jnp.einsum(
        "sjcd,jdf->sjcf", slots_in, expert_gate, preferred_element_type=jnp.float32
    )
    up_val = jnp.einsum("sjcd,jdf->sjcf", slots_in, expert_up, preferred_element_type=jnp.float32)
    inner = (jax.nn.silu(gate_val) * up_val).astype(jnp.bfloat16)
    return jnp.einsum("sjcf,jfd->sjcd", inner, expert_down, preferred_element_type=jnp.float32)


def body(
    hidden,
    norm_gain,
    shared_gate,
    shared_up,
    shared_down,
    expert_gate,
    expert_up,
    expert_down,
    adapter_in,
    adapter_out,
    active,
    lengths,
    request_adapter,
    routes,
    route_weights,
):
    tok_rows = routes.shape[0]
    top_count = routes.shape[1]
    dp_count = lax.axis_size("dp")
    mp_count = lax.axis_size("mp")
    dp_index = lax.axis_index("dp")
    local_experts = expert_gate.shape[0]
    total_experts = local_experts * dp_count
    capacity = mp_count * max(1, tok_rows * top_count * 4 // (total_experts * mp_count * 3))
    gathered = lax.all_gather(hidden, "mp", axis=1, tiled=True)
    values = gathered.astype(jnp.float32)
    factor = lax.rsqrt(jnp.mean(values * values, axis=-1, keepdims=True) + 1e-06)
    normed = (values * factor * norm_gain.astype(jnp.float32)).astype(jnp.bfloat16)
    width = normed.shape[1]
    shared_lin = jnp.dot(normed, shared_gate, preferred_element_type=jnp.float32)
    shared_pre = jnp.dot(normed, shared_up, preferred_element_type=jnp.float32)
    shared_act = (jax.nn.silu(shared_lin) * shared_pre).astype(jnp.bfloat16)
    active_count = active.shape[0]
    rank_width = adapter_in.shape[2]
    local_adapters = adapter_in.shape[0]
    owned_ids = dp_index * local_adapters + jnp.arange(local_adapters, dtype=jnp.int32)
    selector = (active[:, None] == owned_ids[None, :]).astype(jnp.bfloat16)
    picked_in = jnp.einsum(
        "ji,isr->jsr", selector, adapter_in, preferred_element_type=jnp.float32
    ).astype(jnp.bfloat16)
    picked_out = jnp.einsum(
        "ji,ird->jrd", selector, adapter_out, preferred_element_type=jnp.float32
    ).astype(jnp.bfloat16)
    picked_in, picked_out = (
        lax.psum(picked_in, "dp").astype(jnp.float32),
        lax.psum(picked_out, "dp").astype(jnp.float32),
    )
    picked_in = picked_in.astype(jnp.bfloat16)
    request_end = jnp.cumsum(lengths)
    positions = dp_index * tok_rows + jnp.arange(tok_rows, dtype=jnp.int32)
    request_of = jnp.sum((request_end[None, :] <= positions[:, None]).astype(jnp.int32), axis=1)
    request_hot = (
        request_of[:, None] == jnp.arange(lengths.shape[0], dtype=jnp.int32)[None, :]
    ).astype(jnp.int32)
    slot_of = jnp.sum(request_hot * request_adapter[None, :], axis=1)
    chosen = (slot_of[:, None] == jnp.arange(active_count, dtype=jnp.int32)[None, :]).astype(
        jnp.float32
    )
    in_matrix = jnp.transpose(picked_in, (1, 0, 2)).reshape(
        shared_act.shape[1], active_count * rank_width
    )
    lowrank = jnp.dot(shared_act, in_matrix, preferred_element_type=jnp.float32)
    lowrank = (lowrank.reshape(tok_rows, active_count, rank_width) * chosen[:, :, None]).reshape(
        tok_rows, active_count * rank_width
    )
    adapted = jnp.dot(
        lowrank,
        picked_out.reshape(active_count * rank_width, width),
        precision=lax.Precision.HIGHEST,
    )
    partial_out = jnp.dot(shared_act, shared_down, preferred_element_type=jnp.float32) + adapted
    flat_routes = routes.reshape(-1)
    flat_weights = route_weights.reshape(-1)
    expert_hot = (
        flat_routes[:, None] == jnp.arange(total_experts, dtype=jnp.int32)[None, :]
    ).astype(jnp.int32)
    earlier = jnp.cumsum(expert_hot, axis=0) - expert_hot
    position = jnp.sum(earlier * expert_hot, axis=1)
    slot_index = flat_routes * capacity + position
    token_of = jnp.arange(tok_rows * top_count, dtype=jnp.int32) // top_count
    send_rows = (
        jnp.zeros((total_experts * capacity, width), jnp.bfloat16)
        .at[slot_index]
        .set(normed[token_of])
    )
    send_rows = send_rows.reshape(dp_count, local_experts, capacity, width)
    returned = lax.all_to_all(
        experts_apply(
            lax.all_to_all(send_rows, "dp", split_axis=0, concat_axis=0, tiled=True),
            expert_gate,
            expert_up,
            expert_down,
        ).astype(jnp.bfloat16),
        "dp",
        split_axis=0,
        concat_axis=0,
        tiled=True,
    ).astype(jnp.float32)
    returned = returned.reshape(total_experts * capacity, width)
    picked_rows = returned[slot_index]
    routed = jnp.sum(
        (picked_rows * flat_weights[:, None]).reshape(tok_rows, top_count, width), axis=1
    )
    partial_out = partial_out + routed
    return lax.psum_scatter(partial_out.astype(jnp.bfloat16), "mp", scatter_dimension=1, tiled=True)


def solution(mesh):
    in_specs = (
        P("dp", "mp"),
        P(),
        P(None, "mp"),
        P(None, "mp"),
        P("mp", None),
        P("dp", None, "mp"),
        P("dp", None, "mp"),
        P("dp", "mp", None),
        P("dp", "mp", None),
        P("dp", None, None),
        P(),
        P(),
        P(),
        P("dp", None),
        P("dp", None),
    )
    out_specs = P("dp", "mp")
    return jax.shard_map(body, mesh=mesh, in_specs=in_specs, out_specs=out_specs, check_vma=False)
```

profile of v0, /device:TPU:0, one launch (start us, length us, event | category | flops | bytes accessed | tf_op | source)
XLA Modules:
  0.0 373.1 jit_solution(8138706086236999893)
XLA Ops:
  6.5 0.8 copy.48
  7.4 0.1 eq.81
  7.5 0.1 eq.77
  7.6 0.7 broadcast_multiply_fusion
  8.4 1.8 reduce-window.19
  10.2 0.3 slice_reduce_fusion
  10.5 0.1 copy.47
  10.6 0.1 mul.98
  10.8 14.9 %all_gather.3 = bf16[128,2560]{1,0:T(8,128)(2,1)S(1)} all-gather(bf16[128,640]{1,0:T(8,128)(2,1)} %param.15), channel_id=1, replica_groups=mesh['dp'=32,'mp'=4] {'mp'}, dimensions={1}, use_global_device_ids=true | all-gather | bytes 819200 | tf_op jit(solution)/shard_map/all_gather | solution.py:41
  25.7 0.2 fusion.25
  25.9 0.7 convert_element_type.54
  26.6 0.1 fusion.34
  26.8 0.2 fusion.27
  27.0 27.6 %scatter_custom_fusion = bf16[1024,2560]{1,0:T(8,128)(2,1)} fusion(s32[768]{0:T(1024)S(1)} %fusion.40, bf16[128,2560]{1,0:T(8,128)(2,1)S(1)} %fusion.27, s32[1024]{0:T(1024)S(1)} %pad_clamp_fusion.1, bf16[]{:T(256)} %constant.44.clone.1), kind=kCustom, calls=%fused_computation.14 | custom fusion | bytes 5242882 | tf_op jit(solution)/shard_map/scatter | solution.py:100
  54.6 69.7 %all_to_all.10 = bf16[32,2,16,2560]{3,2,1,0:T(8,128)(2,1)S(1)} all-to-all(bf16[32,2,16,2560]{3,2,1,0:T(8,128)(2,1)} %bitcast.96), channel_id=1, replica_groups=mesh['dp'=32,'mp'=4] {'dp'}, dimensions={0} | all-to-all | bytes 10485760 | tf_op jit(solution)/shard_map/all_to_all | solution.py:105
  124.3 2.3 copy-done.2
  126.6 2.9 fusion.3
  129.5 12.8 %fusion = bf16[32,2,16,2560]{3,2,0,1:T(8,128)(2,1)} fusion(bf16[2,384,2560]{2,1,0:T(8,128)(2,1)} %param.22, f32[2,32,16,384]{3,2,1,0:T(8,128)S(1)} %fusion.3, bf16[2,2560,384]{2,1,0:T(8,128)(2,1)} %param.21, bf16[32,2,16,2560]{3,2,1,0:T(8,128)(2,1)} %copy-done.2), kind=kOutput, calls=%fused_computation.6 | convolution fusion | flops 4031512576 | bytes 19922944 | tf_op jit(solution)/shard_map/sjcf,jfd->sjcd/dot_general | solution.py:13
  142.3 5.3 %copy.53 = bf16[32,2,16,2560]{3,2,1,0:T(8,128)(2,1)} copy(bf16[32,2,16,2560]{3,2,0,1:T(8,128)(2,1)} %fusion) | data formatting | bytes 10485760 | tf_op jit(solution)/shard_map/convert_element_type | solution.py:109
  147.6 5.0 %all-to-all-start.1 = ((bf16[32,2,16,2560]{3,2,1,0:T(8,128)(2,1)}), bf16[32,2,16,2560]{3,2,1,0:T(8,128)(2,1)}, u32[]{:S(2)}, u32[]{:S(2)}) async-start(bf16[32,2,16,2560]{3,2,1,0:T(8,128)(2,1)} %copy.53), calls=%async_computation.1 | async-start | bytes 10485760 | tf_op jit(solution)/shard_map/all_to_all | solution.py:103
  152.6 0.0 copy-start.7
  152.6 0.0 all-reduce.3.cloned.1.call-start
  152.7 0.4 fusion.29
  153.1 0.9 copy.77
  154.0 1.7 convolution_convert_fusion.1
  155.8 0.0 all-reduce.3.cloned.1.call-update
  155.8 0.3 reduce-scatter.4.cloned.1.call-start
  156.1 0.1 copy.44
  156.2 0.1 reduce-window.18
  156.3 0.1 reduce
  156.4 0.1 convert_reduce_fusion
  156.5 0.1 select_reduce_fusion
  156.6 0.1 copy.54
  156.7 2.9 fusion.51
  159.7 0.3 copy-done.9
  160.0 0.7 fusion.30
  160.7 138.1 %all-reduce.3.cloned.1.call-done = (bf16[16,16,768]{2,1,0:T(8,128)(2,1)}, bf16[16,16,2560]{2,0,1:T(8,128)(2,1)}) async-done(((bf16[16,16,768]{2,1,0:T(8,128)(2,1)}, bf16[16,16,2560]{2,0,1:T(8,128)(2,1)}), (bf16[16,16,768]{2,1,0:T(8,128)(2,1)}, bf16[16,16,2560]{2,0,1:T(8,128)(2,1)})) %all-reduce.3.cloned.1.call-update) | async-done | bytes 1703952 | tf_op jit(solution)/shard_map/psum | solution.py:61
  298.8 1.3 convolution_multiply_fusion.1
  300.1 2.6 convolution_bitcast_fusion
  302.8 7.9 %bitcast_convert_fusion = f32[1024,2560]{1,0:T(8,128)} fusion(bf16[32,2,16,2560]{3,2,1,0:T(8,128)(2,1)} %all-to-all-done.1), kind=kLoop, calls=%fused_computation.5 | loop fusion | flops 2621440 | bytes 15728640 | tf_op jit(solution)/shard_map/reshape | solution.py:115
  310.7 12.4 %gather_fusion = f32[768,2560]{1,0:T(8,128)} fusion(f32[1024,2560]{1,0:T(8,128)} %bitcast_convert_fusion, s32[1024]{0:T(1024)S(1)} %pad_clamp_fusion), kind=kCustom, calls=%fused_computation.1 | custom fusion | bytes 15731712 | tf_op jit(solution)/shard_map/gather | solution.py:116
  323.1 9.2 %gather.10 = f32[128,6,2560]{2,1,0:T(8,128)} reshape(f32[768,2560]{1,0:T(8,128)} %gather_fusion) | data formatting | bytes 15728640 | tf_op jit(solution)/shard_map/gather | solution.py:116
  332.3 8.1 %multiply_reduce_fusion = f32[128,2560]{1,0:T(8,128)S(1)} fusion(f32[128,6,2560]{2,1,0:T(8,128)} %gather.10, f32[128,6]{1,0:T(8,128)S(1)} %copy.54), kind=kLoop, calls=%fused_computation.3 | loop fusion | flops 3604480 | bytes 9178112 | tf_op jit(solution)/shard_map/reduce_sum | solution.py:117
  340.4 0.7 fusion.11
  341.1 1.1 copy.58
  342.2 0.0 reduce-scatter.4.cloned.1.call-update
  342.2 22.3 %reduce-scatter.4.cloned.1.call-done = bf16[640,128]{1,0:T(8,128)(2,1)} async-done(((bf16[2560,128]{1,0:T(8,128)(2,1)}), bf16[640,128]{1,0:T(8,128)(2,1)}) %reduce-scatter.4.cloned.1.call-update) | async-done | bytes 163856
  364.5 1.7 copy.59
  (30 shorter events, 0.2 us)
Async XLA Ops:
  6.5 147.5 %copy-start = (bf16[2,16,2560]{2,1,0:T(8,128)(2,1)S(1)}, bf16[2,16,2560]{2,1,0:T(8,128)(2,1)}, u32[]{:S(2)}) copy-start(bf16[2,16,2560]{2,1,0:T(8,128)(2,1)} %param.24) | copy-start | bytes 491524
  54.5 72.0 %copy-start.8 = (bf16[2,2560,384]{2,1,0:T(8,128)(2,1)S(1)}, bf16[2,2560,384]{2,1,0:T(8,128)(2,1)}, u32[]{:S(2)}) copy-start(bf16[2,2560,384]{2,1,0:T(8,128)(2,1)} %param.20) | copy-start | bytes 11796484
  124.3 2.3 copy-start.2
  147.6 5.1 %copy-start.4 = (bf16[2,768,16]{1,2,0:T(8,128)(2,1)S(1)}, bf16[2,768,16]{1,2,0:T(8,128)(2,1)}, u32[]{:S(2)}) copy-start(bf16[2,768,16]{1,2,0:T(8,128)(2,1)} %param.23) | copy-start | bytes 147460
  147.6 5.1 %copy-start.6 = (s32[16]{0:T(128)S(1)}, s32[16]{0:T(128)}, u32[]{:S(2)}) copy-start(s32[16]{0:T(128)} %param.25) | copy-start | bytes 196
  147.6 155.2 %all-to-all-start.1 = ((bf16[32,2,16,2560]{3,2,1,0:T(8,128)(2,1)}), bf16[32,2,16,2560]{3,2,1,0:T(8,128)(2,1)}, u32[]{:S(2)}, u32[]{:S(2)}) async-start(bf16[32,2,16,2560]{3,2,1,0:T(8,128)(2,1)} %copy.53), calls=%async_computation.1 | async-start | bytes 10485760 | tf_op jit(solution)/shard_map/all_to_all | solution.py:103
  152.6 3.5 copy-start.7
  152.6 3.9 %copy-start.10 = (s32[64]{0:T(128)S(1)}, s32[64]{0:T(128)}, u32[]{:S(2)}) copy-start(s32[64]{0:T(128)} %param.27) | copy-start | bytes 772
  152.6 4.0 %copy-start.5 = (f32[128,6]{0,1:T(8,128)S(1)}, f32[128,6]{0,1:T(8,128)}, u32[]{:S(2)}) copy-start(f32[128,6]{0,1:T(8,128)} %param.29) | copy-start | bytes 9220
  152.6 146.2 %all-reduce.3.cloned.1.call-start = ((), (), s32[]{:S(2)}) async-start(), calls=%async_computation.4 | async-start | bytes 3407872 | tf_op jit(solution)/shard_map/psum | solution.py:61
  155.8 208.7 %reduce-scatter.4.cloned.1.call-start = ((), (), s32[]{:S(2)}) async-start(), calls=%async_computation.3 | async-start | bytes 819200
  156.7 3.3 copy-start.9
  332.3 8.1 %copy-start.3 = (bf16[768,2560]{1,0:T(8,128)(2,1)S(1)}, bf16[768,2560]{1,0:T(8,128)(2,1)}, u32[]{:S(2)}) copy-start(bf16[768,2560]{1,0:T(8,128)(2,1)} %param.19) | copy-start | bytes 11796484
  332.3 33.9 %copy-start.1 = (bf16[2,16,2560]{2,1,0:T(8,128)(2,1)S(1)}, bf16[2,16,2560]{2,1,0:T(8,128)(2,1)}, u32[]{:S(2)}) copy-start(bf16[2,16,2560]{2,1,0:T(8,128)(2,1)} %param.24) | copy-start | bytes 491524
Sparse Core Ops, SparseCore 0:
  156.8 141.9 all-reduce.2
  342.4 22.1 reduce-scatter.3
where the time goes:
time: 374 us; the launch traced here: 373 us
  waiting for transfers between devices  160 us (43%)
  blocking collectives  84.6 us (23%)
  local copies, waits for them, and re-layouts  62.7 us (17%)
  matrix products  26.1 us (7%)
  other arithmetic  20.3 us (5%)
  between operations  13.6 us (4%)
  starting transfers between devices  5.31 us (1%)
    psum x1, waiting for transfers between devices, body(): lax.psum(picked_in, 'dp').astype(jnp.float32)  138 us
    all_to_all x1, blocking collectives, body(): lax.all_to_all(send_rows, 'dp', split_axis=0, concat_axis=0, tiled=True)  69.7 us
    scatter x1, local copies, waits for them, and re-layouts, body(): send_rows = jnp.zeros((total_experts * capacity, width), jnp.bfloat16).at...  27.6 us
    unnamed x3, waiting for transfers between devices  22.3 us
    gather x2, local copies, waits for them, and re-layouts, body(): picked_rows = returned[slot_index]  21.6 us
    all_gather x1, blocking collectives, body(): gathered = lax.all_gather(hidden, 'mp', axis=1, tiled=True)  14.9 us
    dot_general x1, matrix products, experts_apply(): jnp.einsum('sjcf,jfd->sjcd', inner, expert_down, preferred_element_type=j...  12.8 us
    reduce_sum x1, other arithmetic, body(): jnp.sum((picked_rows * flat_weights[:, None]).reshape(tok_rows, top_count...  8.08 us
  transfers between devices with their start and end apart: 3, of which 2 were waited for; matrix products, arithmetic and copies ran while one was open for 3% of the time, Pallas kernels for 0%

commit v1 on v0

--- a/solution.py
+++ b/solution.py
@@ -58,7 +58,7 @@
         "ji,ird->jrd", selector, adapter_out, preferred_element_type=jnp.float32
     ).astype(jnp.bfloat16)
     picked_in, picked_out = (
-        lax.psum(picked_in, "dp").astype(jnp.float32),
+        jnp.sum(lax.all_gather(picked_in, "dp"), axis=0).astype(jnp.float32),
         lax.psum(picked_out, "dp").astype(jnp.float32),
     )
     picked_in = picked_in.astype(jnp.bfloat16)

time: 374 us -> 344 us (0.920)
  waiting for transfers between devices: 160 us -> 115 us
  other arithmetic: 20.3 us -> 26.4 us
  blocking collectives: 84.6 us -> 89.5 us
    psum x1, waiting for transfers between devices: 138 us -> 31.8 us  [body(): lax.psum(picked_out, 'dp').astype(jnp.float32)]
    all_to_all x1, waiting for transfers between devices: 0.01 us -> 61.2 us  [body(): lax.all_to_all(experts_apply(lax.all_to_all(send_rows, 'dp', split_axis=0...]
    reduce_sum x0 -> x1, other arithmetic: none -> 6.27 us  [body(): jnp.sum(lax.all_gather(picked_in, 'dp'), axis=0).astype(jnp.float32)]
    all_to_all x1, blocking collectives: 69.7 us -> 74.6 us  [body(): lax.all_to_all(send_rows, 'dp', split_axis=0, concat_axis=0, tiled=True)]
    unnamed x3 -> x4, waiting for transfers between devices: 22.3 us -> 22.4 us
  transfers between devices with their start and end apart: 3 -> 4, of which waited for: 2 -> 3; matrix products, arithmetic and copies ran while one was open for 3% -> 31% of each run, Pallas kernels for 0% -> 0%
where the time goes in v1:
time: 344 us; the launch traced here: 341 us
  waiting for transfers between devices  115 us (33%)
  blocking collectives  89.5 us (26%)
  local copies, waits for them, and re-layouts  62.3 us (18%)
  matrix products  28.9 us (8%)
  other arithmetic  26.4 us (8%)
  between operations  13.5 us (4%)
  starting transfers between devices  5.11 us (1%)
    all_to_all x1, blocking collectives, body(): lax.all_to_all(send_rows, 'dp', split_axis=0, concat_axis=0, tiled=True)  74.6 us
    all_to_all x1, waiting for transfers between devices, body(): lax.all_to_all(experts_apply(lax.all_to_all(send_rows, 'dp', split_axis=0...  61.2 us
    psum x1, waiting for transfers between devices, body(): lax.psum(picked_out, 'dp').astype(jnp.float32)  31.8 us
    scatter x1, local copies, waits for them, and re-layouts, body(): send_rows = jnp.zeros((total_experts * capacity, width), jnp.bfloat16).at...  28 us
    unnamed x4, waiting for transfers between devices  22.4 us
    gather x2, local copies, waits for them, and re-layouts, body(): picked_rows = returned[slot_index]  22 us
    all_gather x1, blocking collectives, body(): gathered = lax.all_gather(hidden, 'mp', axis=1, tiled=True)  14.9 us
    dot_general x1, matrix products, experts_apply(): jnp.einsum('sjcf,jfd->sjcd', inner, expert_down, preferred_element_type=j...  12.8 us
  transfers between devices with their start and end apart: 4, of which 3 were waited for; matrix products, arithmetic and copies ran while one was open for 31% of the time, Pallas kernels for 0%

profile of v1, /device:TPU:0, one launch (start us, length us, event | category | flops | bytes accessed | tf_op | source)
XLA Modules:
  0.0 341.1 jit_solution(459571135451095140)
XLA Ops:
  6.5 2.0 convolution_convert_fusion.2
  8.6 0.0 all-gather.3.cloned.1.call-update
  8.6 0.8 copy.47
  9.4 0.1 eq.81
  9.5 0.1 eq.77
  9.7 1.8 reduce-window.19
  11.5 0.3 slice_reduce_fusion
  11.8 0.7 broadcast_multiply_fusion
  12.5 0.1 copy.46
  12.6 0.1 mul.98
  12.8 0.7 convert_element_type.56
  13.5 0.1 fusion.35
  13.7 14.9 %all_gather.9 = bf16[128,2560]{1,0:T(8,128)(2,1)S(1)} all-gather(bf16[128,640]{1,0:T(8,128)(2,1)} %param.15), channel_id=1, replica_groups=mesh['dp'=32,'mp'=4] {'mp'}, dimensions={1}, use_global_device_ids=true | all-gather | bytes 819200 | tf_op jit(solution)/shard_map/all_gather | solution.py:41
  28.6 0.2 fusion.25
  28.8 0.2 fusion.27
  29.0 28.0 %scatter_custom_fusion = bf16[1024,2560]{1,0:T(8,128)(2,1)} fusion(s32[768]{0:T(1024)S(1)} %fusion.41, bf16[128,2560]{1,0:T(8,128)(2,1)S(1)} %fusion.27, s32[1024]{0:T(1024)S(1)} %pad_clamp_fusion.1, bf16[]{:T(256)} %constant.43.clone.1), kind=kCustom, calls=%fused_computation.14 | custom fusion | bytes 5242882 | tf_op jit(solution)/shard_map/scatter | solution.py:100
  57.0 74.6 %all_to_all.10 = bf16[32,2,16,2560]{3,2,1,0:T(8,128)(2,1)S(1)} all-to-all(bf16[32,2,16,2560]{3,2,1,0:T(8,128)(2,1)} %bitcast.95), channel_id=1, replica_groups=mesh['dp'=32,'mp'=4] {'dp'}, dimensions={0} | all-to-all | bytes 10485760 | tf_op jit(solution)/shard_map/all_to_all | solution.py:105
  131.6 2.3 copy-done.2
  133.9 2.9 fusion.3
  136.8 12.8 %fusion = bf16[32,2,16,2560]{3,2,0,1:T(8,128)(2,1)} fusion(bf16[2,384,2560]{2,1,0:T(8,128)(2,1)} %param.22, f32[2,32,16,384]{3,2,1,0:T(8,128)S(1)} %fusion.3, bf16[2,2560,384]{2,1,0:T(8,128)(2,1)} %param.21, bf16[32,2,16,2560]{3,2,1,0:T(8,128)(2,1)} %copy-done.2), kind=kOutput, calls=%fused_computation.6 | convolution fusion | flops 4031512576 | bytes 19922944 | tf_op jit(solution)/shard_map/sjcf,jfd->sjcd/dot_general | solution.py:13
  149.5 5.2 %copy.52 = bf16[32,2,16,2560]{3,2,1,0:T(8,128)(2,1)} copy(bf16[32,2,16,2560]{3,2,0,1:T(8,128)(2,1)} %fusion) | data formatting | bytes 10485760 | tf_op jit(solution)/shard_map/convert_element_type | solution.py:109
  154.8 5.0 %all-to-all-start.1 = ((bf16[32,2,16,2560]{3,2,1,0:T(8,128)(2,1)}), bf16[32,2,16,2560]{3,2,1,0:T(8,128)(2,1)}, u32[]{:S(2)}, u32[]{:S(2)}) async-start(bf16[32,2,16,2560]{3,2,1,0:T(8,128)(2,1)} %copy.52), calls=%async_computation.1 | async-start | bytes 10485760 | tf_op jit(solution)/shard_map/all_to_all | solution.py:103
  159.8 0.0 all-reduce.2.cloned.1.call-start
  159.9 1.7 convolution_convert_fusion.1
  161.7 0.0 reduce-scatter.4.cloned.1.call-start
  161.7 0.1 copy.53
  161.8 0.1 copy.43
  161.9 0.1 reduce-window.18
  162.0 0.1 reduce.1
  162.2 0.1 convert_reduce_fusion
  162.3 0.1 select_reduce_fusion
  162.4 2.9 fusion.52
  165.3 0.1 copy-done.7
  165.4 0.7 fusion.29
  166.1 61.2 %all-to-all-done.1 = bf16[32,2,16,2560]{3,2,1,0:T(8,128)(2,1)} async-done(((bf16[32,2,16,2560]{3,2,1,0:T(8,128)(2,1)}), bf16[32,2,16,2560]{3,2,1,0:T(8,128)(2,1)}, u32[]{:S(2)}, u32[]{:S(2)}) %all-to-all-start.1) | async-done | bytes 5242912 | tf_op jit(solution)/shard_map/all_to_all | solution.py:103
  227.3 7.9 %bitcast_convert_fusion = f32[1024,2560]{1,0:T(8,128)} fusion(bf16[32,2,16,2560]{3,2,1,0:T(8,128)(2,1)} %all-to-all-done.1), kind=kLoop, calls=%fused_computation.5 | loop fusion | flops 2621440 | bytes 15728640 | tf_op jit(solution)/shard_map/reshape | solution.py:115
  235.2 12.7 %gather_fusion = f32[768,2560]{1,0:T(8,128)} fusion(f32[1024,2560]{1,0:T(8,128)} %bitcast_convert_fusion, s32[1024]{0:T(1024)S(1)} %pad_clamp_fusion), kind=kCustom, calls=%fused_computation.1 | custom fusion | bytes 15731712 | tf_op jit(solution)/shard_map/gather | solution.py:116
  247.9 9.3 %gather.10 = f32[128,6,2560]{2,1,0:T(8,128)} reshape(f32[768,2560]{1,0:T(8,128)} %gather_fusion) | data formatting | bytes 15728640 | tf_op jit(solution)/shard_map/gather | solution.py:116
  257.2 8.0 %multiply_reduce_fusion = f32[128,2560]{1,0:T(8,128)S(1)} fusion(f32[128,6,2560]{2,1,0:T(8,128)} %gather.10, f32[128,6]{1,0:T(8,128)S(1)} %copy.53), kind=kLoop, calls=%fused_computation.3 | loop fusion | flops 3604480 | bytes 9178112 | tf_op jit(solution)/shard_map/reduce_sum | solution.py:117
  265.2 0.0 all-gather.3.cloned.1.call-done
  265.2 6.3 %reduce_sum.60 = bf16[16,768,16]{1,0,2:T(8,128)(2,1)S(1)} reduce(bf16[32,16,768,16]{2,1,0,3:T(8,128)(2,1)} %bitcast.96, bf16[]{:T(256)} %constant.43.clone.1), dimensions={0}, to_apply=%region_1.2 | reduce | flops 6094848 | bytes 12976130 | tf_op jit(solution)/shard_map/reduce_sum | solution.py:61
  271.5 0.3 convolution_multiply_fusion.1
  271.8 31.8 %all-reduce.2.cloned.1.call-done = bf16[16,16,2560]{2,0,1:T(8,128)(2,1)} async-done(((bf16[16,16,2560]{2,0,1:T(8,128)(2,1)}), bf16[16,16,2560]{2,0,1:T(8,128)(2,1)}) %all-reduce.2.cloned.1.call-update) | async-done | bytes 1310736 | tf_op jit(solution)/shard_map/psum | solution.py:62
  303.6 2.7 convolution_bitcast_fusion
  306.3 2.9 fusion.11
  309.2 1.1 copy.57
  310.3 22.4 %reduce-scatter.4.cloned.1.call-done = bf16[640,128]{1,0:T(8,128)(2,1)} async-done(((bf16[2560,128]{1,0:T(8,128)(2,1)}), bf16[640,128]{1,0:T(8,128)(2,1)}) %reduce-scatter.4.cloned.1.call-update) | async-done | bytes 163856
  332.7 1.7 copy.58
  (29 shorter events, 0.2 us)
Async XLA Ops:
  6.5 153.3 %copy-start = (bf16[2,16,2560]{2,1,0:T(8,128)(2,1)S(1)}, bf16[2,16,2560]{2,1,0:T(8,128)(2,1)}, u32[]{:S(2)}) copy-start(bf16[2,16,2560]{2,1,0:T(8,128)(2,1)} %param.24) | copy-start | bytes 491524
  6.5 258.7 %all-gather.3.cloned.1.call-start = ((), (), s32[]{:S(2)}) async-start(), calls=%async_computation.4 | async-start | bytes 12976128 | tf_op jit(solution)/shard_map/all_gather | solution.py:61
  57.0 76.9 %copy-start.6 = (bf16[2,2560,384]{2,1,0:T(8,128)(2,1)S(1)}, bf16[2,2560,384]{2,1,0:T(8,128)(2,1)}, u32[]{:S(2)}) copy-start(bf16[2,2560,384]{2,1,0:T(8,128)(2,1)} %param.20) | copy-start | bytes 11796484
  131.6 2.3 copy-start.2
  154.8 5.1 %copy-start.4 = (s32[16]{0:T(128)S(1)}, s32[16]{0:T(128)}, u32[]{:S(2)}) copy-start(s32[16]{0:T(128)} %param.25) | copy-start | bytes 196
  154.8 6.9 %copy-start.3 = (f32[128,6]{0,1:T(8,128)S(1)}, f32[128,6]{0,1:T(8,128)}, u32[]{:S(2)}) copy-start(f32[128,6]{0,1:T(8,128)} %param.29) | copy-start | bytes 9220
  154.8 7.1 %copy-start.5 = (s32[64]{0:T(128)S(1)}, s32[64]{0:T(128)}, u32[]{:S(2)}) copy-start(s32[64]{0:T(128)} %param.26) | copy-start | bytes 772
  154.8 7.5 %copy-start.8 = (s32[64]{0:T(128)S(1)}, s32[64]{0:T(128)}, u32[]{:S(2)}) copy-start(s32[64]{0:T(128)} %param.27) | copy-start | bytes 772
  154.8 72.6 %all-to-all-start.1 = ((bf16[32,2,16,2560]{3,2,1,0:T(8,128)(2,1)}), bf16[32,2,16,2560]{3,2,1,0:T(8,128)(2,1)}, u32[]{:S(2)}, u32[]{:S(2)}) async-start(bf16[32,2,16,2560]{3,2,1,0:T(8,128)(2,1)} %copy.52), calls=%async_computation.1 | async-start | bytes 10485760 | tf_op jit(solution)/shard_map/all_to_all | solution.py:103
  159.8 143.8 %all-reduce.2.cloned.1.call-start = ((), (), s32[]{:S(2)}) async-start(), calls=%async_computation.3 | async-start | bytes 2621440 | tf_op jit(solution)/shard_map/psum | solution.py:62
  161.7 171.0 %reduce-scatter.4.cloned.1.call-start = ((), (), s32[]{:S(2)}) async-start(), calls=%async_computation.5 | async-start | bytes 819200
  162.1 3.3 copy-start.7
  303.6 30.8 %copy-start.1 = (bf16[2,16,2560]{2,1,0:T(8,128)(2,1)S(1)}, bf16[2,16,2560]{2,1,0:T(8,128)(2,1)}, u32[]{:S(2)}) copy-start(bf16[2,16,2560]{2,1,0:T(8,128)(2,1)} %param.24) | copy-start | bytes 491524
Sparse Core Ops, SparseCore 0:
  9.6 91.3 all-gather.2
  163.9 139.6 all-reduce.1
  310.4 22.2 reduce-scatter.3
